TPU v7x, 256 devices: a whole 4x4x8 slice. The times are simulated.
256 devices in a mesh: dp: 64 (over y, z, core), vocab: 4 (over x).
Axes of the slice: x: 4, y: 4, z: 8, core: 2. Of those that a mesh axis runs over, the one named last changes fastest.
Arguments:
- hidden_rows: bfloat16 [16384, 5120], P('dp'), may hold values from -300 to 300, as said below
- plan_lengths: int32 [64], replicated, may hold values from 1 to 256, 8192 in all
- shard_of_class: int32 [64], replicated, may hold values from 0 to 63, each once
- head_weight: bfloat16 [5120, 3072], P(None, 'vocab'), may hold values from -0.078125 to 0.078125
- teacher_logprobs: bfloat16 [8192, 3072], P('dp', 'vocab'), as said below
Outputs:
- row_grad: bfloat16 [16384, 5120], P('dp')
- row_kl: float32 [8192], P('dp')
Inputs may be any that keep to these rules, and one draw needn't show every extreme that they name: `plan_lengths`: the plan lengths sum to 8192 and the longest is exactly 256. `shard_of_class`: each shard is named once. `hidden_rows`: unused slots hold finite values. `teacher_logprobs`: each row is a log-softmax over the 3072 entries, rounded to bfloat16.
All inputs are finite; a program needn't handle non-finite values.
Results may differ from a plain program's by a relative error of at most 0.0046.
Values may be sent and summed in bfloat16 or wider, within the bound.
No kernel may reach another device: no remote copies, remote signals or barrier semaphores. Data moves between devices by JAX's collectives and lax.ppermute only.
A program may use at most 64 MiB of HBM per device.

v0:
```python
import jax
import jax.numpy as jnp
from jax import lax
from jax.sharding import PartitionSpec as P

loss_scale = 64.0


def divergence(row_block, teacher_block, live_rows, weight):
    logits = jnp.dot(row_block, weight, preferred_element_type=jnp.float32)
    log_teacher = teacher_block.astype(jnp.float32)
    teacher_prob = jnp.exp(log_teacher)
    own_top = jnp.max(logits, axis=1)
    own_mass = jnp.sum(teacher_prob, axis=1)
    own_cross = jnp.sum(teacher_prob * (log_teacher - logits), axis=1)
    row_top = lax.pmax(own_top, "vocab")
    own_total = jnp.sum(jnp.exp(logits - row_top[:, None]), axis=1)
    exp_total, prob_total, cross_term = lax.psum((own_total, own_mass, own_cross), "vocab")
    log_total = row_top + jnp.log(exp_total)
    row_div = (cross_term + prob_total * log_total) * live_rows
    grad_logits = (
        loss_scale
        * (prob_total[:, None] * jnp.exp(logits - log_total[:, None]) - teacher_prob)
        * live_rows[:, None]
    ).astype(jnp.bfloat16)
    partial_grad = lax.dot_general(
        grad_logits, weight, (((1,), (1,)), ((), ())), preferred_element_type=jnp.float32
    )
    hidden_grad = lax.psum(partial_grad, "vocab").astype(jnp.bfloat16)
    return (hidden_grad, row_div)


def body(hidden_rows, plan_lengths, shard_of_class, head_weight, teacher_logprobs):
    shards = lax.axis_size("dp")
    myself = lax.axis_index("dp")
    source_slots = hidden_rows.shape[0]
    feature_width = hidden_rows.shape[1]
    slot_depth = source_slots // shards
    balanced = teacher_logprobs.shape[0]
    offsets = jnp.cumsum(plan_lengths) - plan_lengths
    classes = jnp.arange(shards, dtype=jnp.int32)
    inverse = jnp.sum(
        jnp.where(shard_of_class[None, :] == classes[:, None], classes[None, :], 0), axis=1
    )
    own_offset = offsets[myself]
    column_of = (inverse - own_offset) % shards
    shard_at = shard_of_class[(own_offset + classes) % shards]
    rank_rows = jnp.arange(slot_depth, dtype=jnp.int32)[:, None]
    recv_row = rank_rows * shards + ((inverse[myself] - offsets) % shards)[None, :]
    recv_live = recv_row < plan_lengths[None, :]
    recv_slot = jnp.where(recv_live, (offsets[None, :] + recv_row) // shards, balanced)
    safe_slot = jnp.minimum(recv_slot, balanced - 1).reshape(-1)
    outgoing = jnp.take(hidden_rows.reshape(slot_depth, shards, feature_width), column_of, axis=1)
    arriving = lax.all_to_all(outgoing, "dp", split_axis=1, concat_axis=1, tiled=True)
    flattened = arriving.reshape(slot_depth * shards, feature_width)
    live_rows = recv_live.reshape(-1).astype(jnp.float32)
    teacher_slots = jnp.take(teacher_logprobs, safe_slot, axis=0)
    returning, row_div = divergence(flattened, teacher_slots, live_rows, head_weight)
    row_kl = jnp.zeros((balanced,), jnp.float32).at[recv_slot.reshape(-1)].add(row_div, mode="drop")
    share_width = returning.shape[1]
    returned = lax.all_to_all(
        returning.reshape(slot_depth, shards, share_width),
        "dp",
        split_axis=1,
        concat_axis=1,
        tiled=True,
    )
    grad_share = jnp.take(returned, shard_at, axis=1).reshape(source_slots, share_width)
    return (grad_share, row_kl)


def solution(mesh):
    return jax.shard_map(
        body,
        mesh=mesh,
        in_specs=(P("dp", None), P(), P(), P(None, "vocab"), P("dp", "vocab")),
        out_specs=(P("dp", None), P("dp")),
        check_vma=False,
    )
```

profile of v0, /device:TPU:1, one launch (start us, length us, event | category | flops | bytes accessed | tf_op | source)
XLA Modules:
  0.0 298.8 jit_solution(14799237197427120690)
XLA Ops:
  0.6 0.0 copy-start
  0.6 0.8 select_reduce_fusion
  1.5 0.8 copy.15
  2.2 0.1 reduce-window.9
  2.3 0.1 reduce
  2.4 0.6 dynamic_slice.6
  3.0 1.3 and_select_fusion.4
  4.3 0.6 dynamic_slice.7
  4.9 0.7 compare_and_fusion.1
  5.6 3.8 %copy.16 = bf16[4,64,5120]{2,0,1:T(4,128)(2,1)S(1)} copy(bf16[4,64,5120]{2,1,0:T(8,128)(2,1)} %bitcast.18) | data formatting | bytes 5242880 | tf_op jit(solution)/shard_map/reshape | solution.py:53
  9.3 4.2 %gather_fusion.2 = bf16[64,4,5120]{2,1,0:T(4,128)(2,1)} fusion(bf16[4,64,5120]{2,0,1:T(4,128)(2,1)S(1)} %copy.16, s32[1024]{0:T(1024)S(1)} %pad_clamp_fusion.1), kind=kCustom, calls=%fused_computation.clone | custom fusion | bytes 5243136 | tf_op jit(solution)/shard_map/jit(_take)/gather | solution.py:53
  13.5 4.5 %select_bitcast_fusion.1 = bf16[4,64,5120]{2,0,1:T(4,128)(2,1)} fusion(bf16[64,4,5120]{2,1,0:T(4,128)(2,1)} %gather_fusion.2, pred[64]{0:T(512)(128)(4,1)S(1)} %get-tuple-element.14), kind=kLoop, calls=%fused_computation.6 | loop fusion | flops 1310720 | bytes 5242944 | tf_op jit(solution)/shard_map/jit(_take)/select_n | solution.py:53
  18.0 0.0 copy-start.2
  18.0 13.3 %all-to-all-start = ((bf16[4,64,5120]{2,0,1:T(4,128)(2,1)}), bf16[4,64,5120]{2,0,1:T(4,128)(2,1)S(1)}, u32[]{:S(2)}, u32[]{:S(2)}) async-start(bf16[4,64,5120]{2,0,1:T(4,128)(2,1)} %select_bitcast_fusion.1), calls=%async_computation | async-start | bytes 5242880 | tf_op jit(solution)/shard_map/all_to_all | solution.py:54
  31.3 0.1 add_add_fusion
  31.4 0.1 add.183
  31.5 0.1 add.185
  31.5 0.0 copy-done.2
  31.5 0.1 add_compare_fusion
  31.6 0.1 lt.100
  31.7 0.1 lt.102
  31.8 0.0 copy-done
  31.8 1.2 gather_fusion
  33.1 60.5 %all-to-all-done = bf16[4,64,5120]{2,0,1:T(4,128)(2,1)S(1)} async-done(((bf16[4,64,5120]{2,0,1:T(4,128)(2,1)}), bf16[4,64,5120]{2,0,1:T(4,128)(2,1)S(1)}, u32[]{:S(2)}, u32[]{:S(2)}) %all-to-all-start) | async-done | bytes 2621472 | tf_op jit(solution)/shard_map/all_to_all | solution.py:54
  93.5 0.8 copy.17
  94.3 5.5 %fusion.19 = (f32[256]{0:T(256)S(1)}, f32[256,768]{1,0:T(8,128)S(1)}) fusion(bf16[256,5120]{1,0:T(8,128)(2,1)S(1)} %bitcast.21, bf16[5120,768]{1,0:T(8,128)(2,1)} %param.10), kind=kOutput, calls=%fused_computation.66 | convolution fusion | flops 2013462272 | bytes 11273216 | tf_op jit(solution)/shard_map/dot_general | solution.py:10
  99.9 8.5 %pmax.7 = f32[256]{0:T(256)S(1)} all-reduce(f32[256]{0:T(256)S(1)} %get-tuple-element.16), channel_id=1, replica_groups=mesh['dp'=64,'vocab'=4] {'vocab'}, use_global_device_ids=true, to_apply=%region_5.7 | all-reduce | flops 256 | bytes 2048 | tf_op jit(solution)/shard_map/pmax | solution.py:16
  108.3 0.6 fusion.5
  108.9 6.2 %all-reduce.1 = (f32[256]{0:T(256)S(1)}, f32[256]{0:T(256)S(1)}) all-reduce(f32[256]{0:T(256)S(1)} %get-tuple-element.4, f32[256]{0:T(256)S(1)} %get-tuple-element.5), channel_id=1, replica_groups=mesh['dp'=64,'vocab'=4] {'vocab'}, use_global_device_ids=true, to_apply=%region_7.9 | all-reduce | flops 512 | bytes 4096 | tf_op jit(solution)/shard_map/psum | solution.py:18
  115.1 8.0 %fusion.6 = f32[256,5120]{1,0:T(8,128)} fusion(bf16[5120,768]{1,0:T(8,128)(2,1)} %param.10, f32[256,768]{1,0:T(8,128)S(1)} %get-tuple-element.17, f32[256]{0:T(256)S(1)} %broadcast_select_fusion.1, f32[256]{0:T(256)S(1)} %log_add_fusion, f32[256]{0:T(256)S(1)} %get-tuple-element.9, bf16[256,768]{1,0:T(8,128)(2,1)S(1)} %gather_fusion, ...), kind=kOutput, calls=%fused_computation.16 | convolution fusion | flops 2014642176 | bytes 14290176 | tf_op jit(solution)/shard_map/dot_general | solution.py:26
  123.1 89.4 %all-reduce.3 = (bf16[256,5120]{1,0:T(8,128)(2,1)S(1)}, f32[256]{0:T(256)S(1)}) all-reduce(f32[256,5120]{1,0:T(8,128)} %fusion.6, f32[256]{0:T(256)S(1)} %get-tuple-element.3), channel_id=1, replica_groups=mesh['dp'=64,'vocab'=4] {'vocab'}, use_global_device_ids=true, to_apply=%region_8.10 | all-reduce | flops 1310976 | bytes 7866368 | tf_op jit(solution)/shard_map/psum | solution.py:29
  212.5 3.5 %copy.18 = bf16[4,64,5120]{2,0,1:T(4,128)(2,1)} copy(bf16[4,64,5120]{2,1,0:T(8,128)(2,1)S(1)} %bitcast.20) | data formatting | bytes 5242880 | tf_op jit(solution)/shard_map/reshape | solution.py:62
  216.0 0.0 copy-start.1
  216.0 11.2 %all-to-all-start.1 = ((bf16[4,64,5120]{2,0,1:T(4,128)(2,1)}), bf16[4,64,5120]{2,0,1:T(4,128)(2,1)S(1)}, u32[]{:S(2)}, u32[]{:S(2)}) async-start(bf16[4,64,5120]{2,0,1:T(4,128)(2,1)} %copy.18), calls=%async_computation.1 | async-start | bytes 5242880 | tf_op jit(solution)/shard_map/all_to_all | solution.py:61
  227.1 0.7 fusion.15
  227.8 0.0 copy-done.1
  227.8 0.8 gather_fusion.1
  228.6 2.8 scatter_custom_fusion
  231.5 57.9 %all-to-all-done.1 = bf16[4,64,5120]{2,0,1:T(4,128)(2,1)S(1)} async-done(((bf16[4,64,5120]{2,0,1:T(4,128)(2,1)}), bf16[4,64,5120]{2,0,1:T(4,128)(2,1)S(1)}, u32[]{:S(2)}, u32[]{:S(2)}) %all-to-all-start.1) | async-done | bytes 2621472 | tf_op jit(solution)/shard_map/all_to_all | solution.py:61
  289.4 4.2 %gather_fusion.3 = bf16[64,4,5120]{2,1,0:T(4,128)(2,1)} fusion(bf16[4,64,5120]{2,0,1:T(4,128)(2,1)S(1)} %all-to-all-done.1, s32[1024]{0:T(1024)S(1)} %pad_clamp_fusion), kind=kCustom, calls=%fused_computation.1.clone | custom fusion | bytes 5243136 | tf_op jit(solution)/shard_map/jit(_take)/gather | solution.py:68
  293.5 3.0 %select_bitcast_fusion = bf16[4,64,5120]{2,0,1:T(4,128)(2,1)S(1)} fusion(bf16[64,4,5120]{2,1,0:T(4,128)(2,1)} %gather_fusion.3, pred[64]{0:T(512)(128)(4,1)S(1)} %compare_and_fusion), kind=kLoop, calls=%fused_computation.5 | loop fusion | flops 1310720 | bytes 5242944 | tf_op jit(solution)/shard_map/jit(_take)/select_n | solution.py:68
  296.5 2.3 copy.19
  (13 shorter events, 0.1 us)
Async XLA Ops:
  0.6 31.2 %copy-start = (bf16[128,768]{1,0:T(8,128)(2,1)S(1)}, bf16[128,768]{1,0:T(8,128)(2,1)}, u32[]{:S(2)}) copy-start(bf16[128,768]{1,0:T(8,128)(2,1)} %param.11) | copy-start | bytes 589828
  18.0 13.5 %copy-start.2 = (s32[64]{0:T(128)S(1)}, s32[64]{0:T(128)}, u32[]{:S(2)}) copy-start(s32[64]{0:T(128)} %param.8) | copy-start | bytes 772
  18.0 75.5 %all-to-all-start = ((bf16[4,64,5120]{2,0,1:T(4,128)(2,1)}), bf16[4,64,5120]{2,0,1:T(4,128)(2,1)S(1)}, u32[]{:S(2)}, u32[]{:S(2)}) async-start(bf16[4,64,5120]{2,0,1:T(4,128)(2,1)} %select_bitcast_fusion.1), calls=%async_computation | async-start | bytes 5242880 | tf_op jit(solution)/shard_map/all_to_all | solution.py:54
  216.0 11.8 %copy-start.1 = (s32[64]{0:T(128)S(1)}, s32[64]{0:T(128)}, u32[]{:S(2)}) copy-start(s32[64]{0:T(128)} %param.9) | copy-start | bytes 772
  216.0 73.4 %all-to-all-start.1 = ((bf16[4,64,5120]{2,0,1:T(4,128)(2,1)}), bf16[4,64,5120]{2,0,1:T(4,128)(2,1)S(1)}, u32[]{:S(2)}, u32[]{:S(2)}) async-start(bf16[4,64,5120]{2,0,1:T(4,128)(2,1)} %copy.18), calls=%async_computation.1 | async-start | bytes 5242880 | tf_op jit(solution)/shard_map/all_to_all | solution.py:61
where the time goes:
time: 299 us
  waiting for transfers between devices  118 us (39%)
  blocking collectives  104 us (35%)
  starting transfers between devices  24.4 us (8%)
  local copies, waits for them, and re-layouts  22.9 us (8%)
  other arithmetic  14.8 us (5%)
  matrix products  13.5 us (5%)
    psum x1, blocking collectives, divergence(): hidden_grad = lax.psum(partial_grad, 'vocab').astype(jnp.bfloat16)  89.4 us
    all_to_all x1, waiting for transfers between devices, body(): lax.all_to_all(outgoing, 'dp', split_axis=1, concat_axis=1, tiled=True)  60.5 us
    all_to_all x1, waiting for transfers between devices, body(): lax.all_to_all(returning.reshape(slot_depth, shards, share_width), 'dp',...  57.9 us
    all_to_all x1, starting transfers between devices, body(): lax.all_to_all(outgoing, 'dp', split_axis=1, concat_axis=1, tiled=True)  13.3 us
    all_to_all x1, starting transfers between devices, body(): lax.all_to_all(returning.reshape(slot_depth, shards, share_width), 'dp',...  11.2 us
    pmax x1, blocking collectives, divergence(): row_top = lax.pmax(own_top, 'vocab')  8.47 us
    dot_general x1, matrix products, divergence(): lax.dot_general(grad_logits, weight, (((1,), (1,)), ((), ())), preferred_...  7.99 us
    psum x1, blocking collectives, divergence(): lax.psum((own_total, own_mass, own_cross), 'vocab')  6.18 us
  transfers between devices with their start and end apart: 2, of which 2 were waited for; matrix products, arithmetic and copies ran while one was open for 2% of the time, Pallas kernels for 0%

commit v1 on v0

--- a/solution.py
+++ b/solution.py
@@ -51,7 +51,9 @@
     recv_slot = jnp.where(recv_live, (offsets[None, :] + recv_row) // shards, balanced)
     safe_slot = jnp.minimum(recv_slot, balanced - 1).reshape(-1)
     outgoing = jnp.take(hidden_rows.reshape(slot_depth, shards, feature_width), column_of, axis=1)
-    arriving = lax.all_to_all(outgoing, "dp", split_axis=1, concat_axis=1, tiled=True)
+    pieces = jnp.split(outgoing, lax.axis_size("dp"), axis=1)
+    incoming = lax.all_to_all(jnp.stack(pieces), "dp", 0, 0)
+    arriving = jnp.concatenate(incoming, axis=1)
     flattened = arriving.reshape(slot_depth * shards, feature_width)
     live_rows = recv_live.reshape(-1).astype(jnp.float32)
     teacher_slots = jnp.take(teacher_logprobs, safe_slot, axis=0)

time: 299 us -> 339 us (1.13)
  local copies, waits for them, and re-layouts: 22.9 us -> 63.4 us
    unnamed x6 -> x69, local copies, waits for them, and re-layouts: 0.02 us -> 39.8 us
where the time goes in v1:
time: 339 us; the launch traced here: 338 us
  waiting for transfers between devices  119 us (35%)
  blocking collectives  104 us (31%)
  local copies, waits for them, and re-layouts  63.4 us (19%)
  starting transfers between devices  24.4 us (7%)
  matrix products  13.5 us (4%)
  other arithmetic  13.3 us (4%)
    psum x1, blocking collectives, divergence(): hidden_grad = lax.psum(partial_grad, 'vocab').astype(jnp.bfloat16)  89.4 us
    all_to_all x1, waiting for transfers between devices, body(): incoming = lax.all_to_all(jnp.stack(pieces), 'dp', 0, 0)  60.4 us
    all_to_all x1, waiting for transfers between devices, body(): lax.all_to_all(returning.reshape(slot_depth, shards, share_width), 'dp',...  58.6 us
    unnamed x69, local copies, waits for them, and re-layouts  39.8 us
    all_to_all x1, starting transfers between devices, body(): incoming = lax.all_to_all(jnp.stack(pieces), 'dp', 0, 0)  13.3 us
    all_to_all x1, starting transfers between devices, body(): lax.all_to_all(returning.reshape(slot_depth, shards, share_width), 'dp',...  11.1 us
    pmax x1, blocking collectives, divergence(): row_top = lax.pmax(own_top, 'vocab')  8.47 us
    dot_general x1, matrix products, divergence(): lax.dot_general(grad_logits, weight, (((1,), (1,)), ((), ())), preferred_...  8 us
  transfers between devices with their start and end apart: 2, of which 2 were waited for; matrix products, arithmetic and copies ran while one was open for 2% of the time, Pallas kernels for 0%

profile of v1, /device:TPU:1, one launch (start us, length us, event | category | flops | bytes accessed | tf_op | source)
XLA Modules:
  0.0 338.3 jit_solution(16366928813156998381)
XLA Ops:
  0.6 0.8 select_reduce_fusion
  1.5 0.8 copy.79
  3.0 1.3 and_select_fusion.4
  4.9 0.7 compare_and_fusion.1
  5.6 0.7 fusion.15
  6.2 3.8 %copy.80 = bf16[4,64,5120]{2,0,1:T(4,128)(2,1)S(1)} copy(bf16[4,64,5120]{2,1,0:T(8,128)(2,1)} %bitcast.276) | data formatting | bytes 5242880 | tf_op jit(solution)/shard_map/reshape | solution.py:53
  10.0 4.2 %gather_fusion.2 = bf16[64,4,5120]{2,1,0:T(4,128)(2,1)} fusion(bf16[4,64,5120]{2,0,1:T(4,128)(2,1)S(1)} %copy.80, s32[1024]{0:T(1024)S(1)} %get-tuple-element.18), kind=kCustom, calls=%fused_computation.clone | custom fusion | bytes 5243136 | tf_op jit(solution)/shard_map/jit(_take)/gather | solution.py:53
  14.2 3.0 select_bitcast_fusion.1
  17.2 0.6 constant_dynamic-update-slice_fusion.63
  17.8 0.6 constant_dynamic-update-slice_fusion.62
  18.5 0.6 constant_dynamic-update-slice_fusion.61
  19.1 0.6 constant_dynamic-update-slice_fusion.60
  19.7 0.6 constant_dynamic-update-slice_fusion.59
  20.3 0.6 constant_dynamic-update-slice_fusion.58
  21.0 0.6 constant_dynamic-update-slice_fusion.57
  21.6 0.6 constant_dynamic-update-slice_fusion.56
  23.5 0.6 constant_dynamic-update-slice_fusion.53
  24.8 0.6 constant_dynamic-update-slice_fusion.51
  27.9 0.6 constant_dynamic-update-slice_fusion.46
  29.2 0.6 constant_dynamic-update-slice_fusion.44
  32.4 0.6 constant_dynamic-update-slice_fusion.39
  35.5 0.6 constant_dynamic-update-slice_fusion.34
  36.8 0.6 constant_dynamic-update-slice_fusion.32
  40.0 0.6 constant_dynamic-update-slice_fusion.27
  41.2 0.6 constant_dynamic-update-slice_fusion.25
  44.4 0.6 constant_dynamic-update-slice_fusion.20
  47.6 0.6 constant_dynamic-update-slice_fusion.15
  48.8 0.6 constant_dynamic-update-slice_fusion.13
  52.0 0.6 constant_dynamic-update-slice_fusion.8
  53.2 0.6 constant_dynamic-update-slice_fusion.6
  56.4 0.6 constant_dynamic-update-slice_fusion.1
  57.7 13.3 %all-to-all-start = ((bf16[64,4,1,5120]{3,1,2,0:T(4,128)(2,1)}), bf16[64,4,1,5120]{3,1,2,0:T(4,128)(2,1)S(1)}, u32[]{:S(2)}, u32[]{:S(2)}) async-start(bf16[64,4,1,5120]{3,1,2,0:T(4,128)(2,1)} %constant_dynamic-update-slice_fusion), calls=%async_computation | async-start | bytes 5242880 | tf_op jit(solution)/shard_map/all_to_all | solution.py:55
  71.5 1.2 gather_fusion
  72.7 60.4 %all-to-all-done = bf16[64,4,1,5120]{3,1,2,0:T(4,128)(2,1)S(1)} async-done(((bf16[64,4,1,5120]{3,1,2,0:T(4,128)(2,1)}), bf16[64,4,1,5120]{3,1,2,0:T(4,128)(2,1)S(1)}, u32[]{:S(2)}, u32[]{:S(2)}) %all-to-all-start) | async-done | bytes 2621472 | tf_op jit(solution)/shard_map/all_to_all | solution.py:55
  133.2 0.8 copy.81
  134.0 5.5 %fusion.19 = (f32[256]{0:T(256)S(1)}, f32[256,768]{1,0:T(8,128)S(1)}) fusion(bf16[256,5120]{1,0:T(8,128)(2,1)S(1)} %bitcast.279, bf16[5120,768]{1,0:T(8,128)(2,1)} %param.10), kind=kOutput, calls=%fused_computation.194 | convolution fusion | flops 2013462272 | bytes 11273216 | tf_op jit(solution)/shard_map/dot_general | solution.py:10
  139.5 8.5 %pmax.7 = f32[256]{0:T(256)S(1)} all-reduce(f32[256]{0:T(256)S(1)} %get-tuple-element.16), channel_id=1, replica_groups=mesh['dp'=64,'vocab'=4] {'vocab'}, use_global_device_ids=true, to_apply=%region_5.7 | all-reduce | flops 256 | bytes 2048 | tf_op jit(solution)/shard_map/pmax | solution.py:16
  148.6 6.0 %all-reduce.1 = (f32[256]{0:T(256)S(1)}, f32[256]{0:T(256)S(1)}) all-reduce(f32[256]{0:T(256)S(1)} %get-tuple-element.4, f32[256]{0:T(256)S(1)} %get-tuple-element.5), channel_id=1, replica_groups=mesh['dp'=64,'vocab'=4] {'vocab'}, use_global_device_ids=true, to_apply=%region_7.9 | all-reduce | flops 512 | bytes 4096 | tf_op jit(solution)/shard_map/psum | solution.py:18
  154.6 8.0 %fusion.6 = f32[256,5120]{1,0:T(8,128)} fusion(bf16[5120,768]{1,0:T(8,128)(2,1)} %param.10, f32[256,768]{1,0:T(8,128)S(1)} %get-tuple-element.17, f32[256]{0:T(256)S(1)} %broadcast_select_fusion.1, f32[256]{0:T(256)S(1)} %log_add_fusion, f32[256]{0:T(256)S(1)} %get-tuple-element.9, bf16[256,768]{1,0:T(8,128)(2,1)S(1)} %gather_fusion, ...), kind=kOutput, calls=%fused_computation.16 | convolution fusion | flops 2014642176 | bytes 14290176 | tf_op jit(solution)/shard_map/dot_general | solution.py:26
  162.6 89.4 %all-reduce.3 = (bf16[256,5120]{1,0:T(8,128)(2,1)S(1)}, f32[256]{0:T(256)S(1)}) all-reduce(f32[256,5120]{1,0:T(8,128)} %fusion.6, f32[256]{0:T(256)S(1)} %get-tuple-element.3), channel_id=1, replica_groups=mesh['dp'=64,'vocab'=4] {'vocab'}, use_global_device_ids=true, to_apply=%region_8.10 | all-reduce | flops 1310976 | bytes 7866368 | tf_op jit(solution)/shard_map/psum | solution.py:29
  252.0 3.5 %copy.82 = bf16[4,64,5120]{2,0,1:T(4,128)(2,1)} copy(bf16[4,64,5120]{2,1,0:T(8,128)(2,1)S(1)} %bitcast.278) | data formatting | bytes 5242880 | tf_op jit(solution)/shard_map/reshape | solution.py:64
  255.5 11.1 %all-to-all-start.1 = ((bf16[4,64,5120]{2,0,1:T(4,128)(2,1)}), bf16[4,64,5120]{2,0,1:T(4,128)(2,1)S(1)}, u32[]{:S(2)}, u32[]{:S(2)}) async-start(bf16[4,64,5120]{2,0,1:T(4,128)(2,1)} %copy.82), calls=%async_computation.1 | async-start | bytes 5242880 | tf_op jit(solution)/shard_map/all_to_all | solution.py:63
  266.6 0.8 gather_fusion.1
  267.5 2.8 scatter_custom_fusion
  270.3 58.6 %all-to-all-done.1 = bf16[4,64,5120]{2,0,1:T(4,128)(2,1)S(1)} async-done(((bf16[4,64,5120]{2,0,1:T(4,128)(2,1)}), bf16[4,64,5120]{2,0,1:T(4,128)(2,1)S(1)}, u32[]{:S(2)}, u32[]{:S(2)}) %all-to-all-start.1) | async-done | bytes 2621472 | tf_op jit(solution)/shard_map/all_to_all | solution.py:63
  328.9 4.2 %gather_fusion.3 = bf16[64,4,5120]{2,1,0:T(4,128)(2,1)} fusion(bf16[4,64,5120]{2,0,1:T(4,128)(2,1)S(1)} %all-to-all-done.1, s32[1024]{0:T(1024)S(1)} %pad_clamp_fusion), kind=kCustom, calls=%fused_computation.1.clone | custom fusion | bytes 5243136 | tf_op jit(solution)/shard_map/jit(_take)/gather | solution.py:70
  333.0 3.0 select_bitcast_fusion
  336.0 2.3 copy.83
  (70 shorter events, 28.5 us)
Async XLA Ops:
  0.6 70.9 %copy-start = (bf16[128,768]{1,0:T(8,128)(2,1)S(1)}, bf16[128,768]{1,0:T(8,128)(2,1)}, u32[]{:S(2)}) copy-start(bf16[128,768]{1,0:T(8,128)(2,1)} %param.11) | copy-start | bytes 589828
  57.7 13.5 %copy-start.2 = (s32[64]{0:T(128)S(1)}, s32[64]{0:T(128)}, u32[]{:S(2)}) copy-start(s32[64]{0:T(128)} %param.8) | copy-start | bytes 772
  57.7 75.5 %all-to-all-start = ((bf16[64,4,1,5120]{3,1,2,0:T(4,128)(2,1)}), bf16[64,4,1,5120]{3,1,2,0:T(4,128)(2,1)S(1)}, u32[]{:S(2)}, u32[]{:S(2)}) async-start(bf16[64,4,1,5120]{3,1,2,0:T(4,128)(2,1)} %constant_dynamic-update-slice_fusion), calls=%async_computation | async-start | bytes 5242880 | tf_op jit(solution)/shard_map/all_to_all | solution.py:55
  255.5 11.1 %copy-start.1 = (s32[64]{0:T(128)S(1)}, s32[64]{0:T(128)}, u32[]{:S(2)}) copy-start(s32[64]{0:T(128)} %param.9) | copy-start | bytes 772
  255.5 73.4 %all-to-all-start.1 = ((bf16[4,64,5120]{2,0,1:T(4,128)(2,1)}), bf16[4,64,5120]{2,0,1:T(4,128)(2,1)S(1)}, u32[]{:S(2)}, u32[]{:S(2)}) async-start(bf16[4,64,5120]{2,0,1:T(4,128)(2,1)} %copy.82), calls=%async_computation.1 | async-start | bytes 5242880 | tf_op jit(solution)/shard_map/all_to_all | solution.py:63
